TPU v7x, 32 devices: a whole 2x2x4 slice. The times are simulated.
32 devices in a mesh: group: 2 (over y), ctx: 4 (over z), head: 2 (over x), sub: 2 (over core).
Axes of the slice: x: 2, y: 2, z: 4, core: 2. Of those that a mesh axis runs over, the one named last changes fastest.
Arguments:
- queries: bfloat16 [4, 4096, 128], P(('head', 'sub'), ('group', 'ctx')), parts along dimension 1, may hold values from -18 to 18
- keys: bfloat16 [4, 4096, 128], P(('head', 'sub'), ('group', 'ctx')), parts along dimension 1, may hold values from -6 to 6
- values: bfloat16 [4, 4096, 128], P(('head', 'sub'), ('group', 'ctx')), parts along dimension 1, may hold values from -6 to 6
- stick_offset: float32 [4], P(('head', 'sub')), may hold values from -14 to -7
Outputs:
- attended: bfloat16 [4, 4096, 128], P(('head', 'sub'), ('group', 'ctx')), parts along dimension 1
There are 2 independent parts, one for each index of `group`. A program takes and returns all parts, laid end to end along the dimension named above; an argument that names none is the same for every part. Nothing has to cross between parts.
All inputs are finite; a program needn't handle non-finite values.
Results may differ from a plain program's by a relative error of at most 0.0049.
Values may be sent and summed in bfloat16 or wider, within the bound.
No kernel may reach another device: no remote copies, remote signals or barrier semaphores. Data moves between devices by JAX's collectives and lax.ppermute only.
A program may use at most 64 MiB of HBM per device.

v0:
```python
import math
import jax
import jax.numpy as jnp
from jax import lax
from jax.sharding import PartitionSpec as P


def shifted(block, axis, distance):
    devices = range(lax.axis_size(axis))
    route = [((i - distance) % len(devices), i) for i in devices]
    return lax.ppermute(block, axis, route)


def shard_terms(qrows, qstart, kblock, vblock, kstart, offset):
    count_rows = qrows.shape[0]
    count_keys = kblock.shape[0]
    width = qrows.shape[1]
    scale = 1.0 / math.sqrt(width)

    def compute(unused):
        score = (
            lax.dot_general(
                qrows, kblock, (((1,), (1,)), ((), ())), preferred_element_type=jnp.float32
            )
            * scale
            + offset
        )
        qpos = qstart + lax.iota(jnp.int32, count_rows)
        kpos = kstart + lax.iota(jnp.int32, count_keys)
        live = kpos[None, :] < qpos[:, None]
        spent = jnp.where(live, jax.nn.softplus(score), 0.0)
        total = jnp.sum(spent, axis=1)
        later = lax.cumsum(spent, axis=1, reverse=True) - spent
        weight = jnp.where(live, jnp.exp(jax.nn.log_sigmoid(score) - later), 0.0).astype(
            jnp.bfloat16
        )
        return (total, jnp.dot(weight, vblock, preferred_element_type=jnp.float32))

    def nothing(unused):
        return (jnp.zeros((count_rows,), jnp.float32), jnp.zeros((count_rows, width), jnp.float32))

    return lax.cond(qstart + count_rows > kstart, compute, nothing, 0)


def one_head(q_own, k_own, v_own, offset):
    rows, width = q_own.shape
    count = lax.axis_size("ctx")
    place = lax.axis_index("ctx")
    own_start = place * rows
    gathered = lax.all_gather(q_own, "ctx", axis=0, tiled=True).reshape(count, rows, width)

    def advance(step, message):
        summed, spent_sum = message
        block = (place + step + 1) % count
        qrows = lax.dynamic_index_in_dim(gathered, block, 0, keepdims=False)
        total, partial_value = shard_terms(qrows, block * rows, k_own, v_own, own_start, offset)
        summed = summed + jnp.exp(-spent_sum)[:, None] * partial_value
        spent_sum = spent_sum + total
        return shifted((summed, spent_sum), "ctx", -1)

    start_message = (jnp.zeros((rows, width), jnp.float32), jnp.zeros((rows,), jnp.float32))
    summed, spent_sum = lax.fori_loop(0, count - 1, advance, start_message)
    total, partial_value = shard_terms(q_own, own_start, k_own, v_own, own_start, offset)
    merged = partial_value + jnp.exp(-total)[:, None] * summed
    return merged.astype(jnp.bfloat16)


def on_device(queries, keys, values, stick_offset):
    results = [one_head(queries[0], keys[0], values[0], stick_offset[0])]
    return jnp.stack(results, axis=0)


def solution(mesh):
    placed = (
        P(("head", "sub"), ("group", "ctx"), None),
        P(("head", "sub"), ("group", "ctx"), None),
        P(("head", "sub"), ("group", "ctx"), None),
        P(("head", "sub")),
    )
    return jax.shard_map(
        on_device,
        mesh=mesh,
        in_specs=placed,
        out_specs=P(("head", "sub"), ("group", "ctx"), None),
        check_vma=False,
    )
```

profile of v0, /device:TPU:0, one launch (start us, length us, event | category | flops | bytes accessed | tf_op | source)
XLA Modules:
  0.0 75.3 jit_solution(1740217966002129003)
XLA Ops:
  0.0 9.7 %conditional.2 = (f32[512]{0:T(512)S(1)}, f32[512,128]{1,0:T(8,128)S(1)}) conditional(s32[]{:T(128)} %convert_element_type.23, () %tuple.48, (s32[]{:T(128)}, bf16[512,128]{1,0:T(8,128)(2,1)}, bf16[512,128]{1,0:T(8,128)(2,1)}, f32[]{:T(128)}, bf16[512,128]{1,0:T(8,128)(2,1)}) %tuple.82), branch_computations={%region_0.1_spmd, %region_1.5_spmd} | conditional | flops 175906304 | bytes 12814392 | solution.py:42
  0.0 2.5 %compare_select_fusion.3 = (f32[512,512]{0,1:T(8,128)S(1)}, f32[512,512]{0,1:T(8,128)S(1)}) fusion(s32[512]{0:T(512)S(1)} %iota_add_fusion, f32[]{:T(128)} %get-tuple-element.273, bf16[512,128]{1,0:T(8,128)(2,1)} %get-tuple-element.271, bf16[512,128]{1,0:T(8,128)(2,1)} %get-tuple-element.272), kind=kOutput, calls=%fused_computation.5 | convolution fusion | flops 69730304 | bytes 2361348 | tf_op jit(solution)/shard_map/cond/branch_1_fun/dot_general | solution.py:22
  2.5 4.8 %fusion.5 = f32[512,4,128]{0,1,2:T(4,128)S(1)} fusion(f32[512,4,128]{0,2,1:T(8,128)S(1)} %bitcast.47), kind=kOutput, calls=%fused_computation.11 | output fusion | flops 33292288 | bytes 2097152 | tf_op jit(solution)/shard_map/reduce-window.2
  7.8 1.5 %fusion.1 = (bf16[512,512]{0,1:T(8,128)(2,1)S(1)}, f32[512]{0:T(512)S(1)}) fusion(f32[512,4,128]{0,2,1:T(8,128)S(1)} %copy.6, f32[512,512]{0,1:T(8,128)S(1)} %get-tuple-element.321, s32[512]{0:T(512)S(1)} %iota_add_fusion), kind=kLoop, calls=%fused_computation.6 | loop fusion | flops 5504512 | bytes 2625536 | tf_op jit(solution)/shard_map/cond/branch_1_fun/convert_element_type | solution.py:34
  9.7 17.8 %all-gather = bf16[1,2048,128]{2,1,0:T(8,128)(2,1)S(1)} all-gather(bf16[1,512,128]{2,1,0:T(8,128)(2,1)} %param.10), channel_id=2, replica_groups=mesh['group'=2,'ctx'=4,'head'=2,'sub'=2] {'ctx'}, dimensions={1}, use_global_device_ids=true | all-gather | bytes 655360 | tf_op jit(solution)/shard_map/all_gather | solution.py:50
  27.5 0.9 %copy-done = bf16[1,512,128]{2,1,0:T(8,128)(2,1)S(1)} copy-done((bf16[1,512,128]{2,1,0:T(8,128)(2,1)S(1)}, bf16[1,512,128]{2,1,0:T(8,128)(2,1)}, u32[]{:S(2)}) %copy-start) | copy-done | bytes 131096
  28.4 46.1 %while.17 = (s32[]{:T(128)}, f32[512,128]{1,0:T(8,128)S(1)}, f32[512]{0:T(512)S(1)}, s32[]{:T(128)}, s32[]{:T(128)}, /*index=5*/bf16[4,512,128]{2,1,0:T(8,128)(2...) while((s32[]{:T(128)}, f32[512,128]{1,0:T(8,128)S(1)}, ...), condition=%wide.region_11.12_spmd, body=%wide.region_5.11_spmd.sunk | while | flops 176038928 | bytes 14150142 | solution.py:62
  28.4 8.7 %conditional.4 = (f32[512]{0:T(512)S(1)}, f32[512,128]{1,0:T(8,128)S(1)}) conditional(s32[]{:T(128)} %convert_element_type.31, () %tuple.69, (s32[]{:T(128)}, s32[]{:T(128)}, s32[]{:T(128)}, bf16[4,512,128]{2,1,0:T(8,128)(2,1)S(1)}, bf16[512,128]{1,0:T(8,128)(2,1)S(1)}, /*index=5*/f32[]{:T(128)}, bf16[512,128]{1,0:T(8,128)(2,1)S(1)}) %tuple.70), branch_computations={%region_6.6_spmd, %region_7.10_spmd} | conditional | flops 175906816 | bytes 12296262 | solution.py:42
  28.4 1.5 %compare_select_fusion.7 = (f32[512,512]{0,1:T(8,128)S(1)}, f32[512,512]{0,1:T(8,128)S(1)}) fusion(s32[512]{0:T(512)S(1)} %get-tuple-element.326, s32[512]{0:T(512)S(1)} %get-tuple-element.327, f32[]{:T(128)} %get-tuple-element.280, bf16[512,128]{1,0:T(8,128)(2,1)S(1)} %get-tuple-element.279, bf16[4,512,128]{2,1,0:T(8,128)(2,1)S(1)} %get-tuple-element.277, ...), kind=kOutput, calls=%fused_computation.22 | convolution fusion | flops 69730304 | bytes 2363400 | tf_op jit(solution)/shard_map/while/body/eval_jaxpr/cond/branch_1_fun/dot_general | solution.py:22
  29.9 4.8 %fusion.13 = f32[512,4,128]{0,1,2:T(4,128)S(1)} fusion(f32[512,4,128]{0,2,1:T(8,128)S(1)} %bitcast.41), kind=kOutput, calls=%fused_computation.28 | output fusion | flops 33292288 | bytes 2097152 | tf_op jit(solution)/shard_map/reduce-window.4
  35.2 1.5 %fusion.9 = (bf16[512,512]{0,1:T(8,128)(2,1)S(1)}, f32[512]{0:T(512)S(1)}) fusion(f32[512,4,128]{0,2,1:T(8,128)S(1)} %copy.8, f32[512,512]{0,1:T(8,128)S(1)} %get-tuple-element.325, s32[512]{0:T(512)S(1)} %get-tuple-element.326, s32[512]{0:T(512)S(1)} %get-tuple-element.327), kind=kLoop, calls=%fused_computation.23 | loop fusion | flops 5504512 | bytes 2627584 | tf_op jit(solution)/shard_map/while/body/eval_jaxpr/cond/branch_1_fun/convert_element_type | solution.py:34
  37.3 2.2 %collective-permute-start.1 = (f32[512]{0:T(512)S(1)}, f32[512]{0:T(512)S(1)}, u32[]{:S(2)}, u32[]{:S(2)}) collective-permute-start(f32[512]{0:T(512)S(1)} %get-tuple-element.392), channel_id=1, source_target_pairs={{4,0},{8,4},{12,8},{0,12},{5,1},{9,5},{13,9},{1,13},{6,2},{10,6},{... | collective-permute-start | bytes 6152 | tf_op jit(solution)/shard_map/while/body/eval_jaxpr/ppermute | solution.py:11
  39.5 4.5 %collective-permute-done.1 = f32[512]{0:T(512)S(1)} collective-permute-done((f32[512]{0:T(512)S(1)}, f32[512]{0:T(512)S(1)}, u32[]{:S(2)}, u32[]{:S(2)}) %collective-permute-start.1) | collective-permute-done | bytes 2080 | tf_op jit(solution)/shard_map/while/body/eval_jaxpr/ppermute | solution.py:11
  44.0 8.7 %conditional.4 = (f32[512]{0:T(512)S(1)}, f32[512,128]{1,0:T(8,128)S(1)}) conditional(s32[]{:T(128)} %convert_element_type.31, () %tuple.69, (s32[]{:T(128)}, s32[]{:T(128)}, s32[]{:T(128)}, bf16[4,512,128]{2,1,0:T(8,128)(2,1)S(1)}, bf16[512,128]{1,0:T(8,128)(2,1)S(1)}, /*index=5*/f32[]{:T(128)}, bf16[512,128]{1,0:T(8,128)(2,1)S(1)}) %tuple.70), branch_computations={%region_6.6_spmd, %region_7.10_spmd} | conditional | flops 175906816 | bytes 12296262 | solution.py:42
  44.0 1.5 %compare_select_fusion.7 = (f32[512,512]{0,1:T(8,128)S(1)}, f32[512,512]{0,1:T(8,128)S(1)}) fusion(s32[512]{0:T(512)S(1)} %get-tuple-element.326, s32[512]{0:T(512)S(1)} %get-tuple-element.327, f32[]{:T(128)} %get-tuple-element.280, bf16[512,128]{1,0:T(8,128)(2,1)S(1)} %get-tuple-element.279, bf16[4,512,128]{2,1,0:T(8,128)(2,1)S(1)} %get-tuple-element.277, ...), kind=kOutput, calls=%fused_computation.22 | convolution fusion | flops 69730304 | bytes 2363400 | tf_op jit(solution)/shard_map/while/body/eval_jaxpr/cond/branch_1_fun/dot_general | solution.py:22
  45.5 4.8 %fusion.13 = f32[512,4,128]{0,1,2:T(4,128)S(1)} fusion(f32[512,4,128]{0,2,1:T(8,128)S(1)} %bitcast.41), kind=kOutput, calls=%fused_computation.28 | output fusion | flops 33292288 | bytes 2097152 | tf_op jit(solution)/shard_map/reduce-window.4
  50.8 1.5 %fusion.9 = (bf16[512,512]{0,1:T(8,128)(2,1)S(1)}, f32[512]{0:T(512)S(1)}) fusion(f32[512,4,128]{0,2,1:T(8,128)S(1)} %copy.8, f32[512,512]{0,1:T(8,128)S(1)} %get-tuple-element.325, s32[512]{0:T(512)S(1)} %get-tuple-element.326, s32[512]{0:T(512)S(1)} %get-tuple-element.327), kind=kLoop, calls=%fused_computation.23 | loop fusion | flops 5504512 | bytes 2627584 | tf_op jit(solution)/shard_map/while/body/eval_jaxpr/cond/branch_1_fun/convert_element_type | solution.py:34
  53.0 6.3 %collective-permute-done.1 = f32[512]{0:T(512)S(1)} collective-permute-done((f32[512]{0:T(512)S(1)}, f32[512]{0:T(512)S(1)}, u32[]{:S(2)}, u32[]{:S(2)}) %collective-permute-start.1) | collective-permute-done | bytes 2080 | tf_op jit(solution)/shard_map/while/body/eval_jaxpr/ppermute | solution.py:11
  59.3 8.7 %conditional.4 = (f32[512]{0:T(512)S(1)}, f32[512,128]{1,0:T(8,128)S(1)}) conditional(s32[]{:T(128)} %convert_element_type.31, () %tuple.69, (s32[]{:T(128)}, s32[]{:T(128)}, s32[]{:T(128)}, bf16[4,512,128]{2,1,0:T(8,128)(2,1)S(1)}, bf16[512,128]{1,0:T(8,128)(2,1)S(1)}, /*index=5*/f32[]{:T(128)}, bf16[512,128]{1,0:T(8,128)(2,1)S(1)}) %tuple.70), branch_computations={%region_6.6_spmd, %region_7.10_spmd} | conditional | flops 175906816 | bytes 12296262 | solution.py:42
  59.3 1.5 %compare_select_fusion.7 = (f32[512,512]{0,1:T(8,128)S(1)}, f32[512,512]{0,1:T(8,128)S(1)}) fusion(s32[512]{0:T(512)S(1)} %get-tuple-element.326, s32[512]{0:T(512)S(1)} %get-tuple-element.327, f32[]{:T(128)} %get-tuple-element.280, bf16[512,128]{1,0:T(8,128)(2,1)S(1)} %get-tuple-element.279, bf16[4,512,128]{2,1,0:T(8,128)(2,1)S(1)} %get-tuple-element.277, ...), kind=kOutput, calls=%fused_computation.22 | convolution fusion | flops 69730304 | bytes 2363400 | tf_op jit(solution)/shard_map/while/body/eval_jaxpr/cond/branch_1_fun/dot_general | solution.py:22
  60.8 4.8 %fusion.13 = f32[512,4,128]{0,1,2:T(4,128)S(1)} fusion(f32[512,4,128]{0,2,1:T(8,128)S(1)} %bitcast.41), kind=kOutput, calls=%fused_computation.28 | output fusion | flops 33292288 | bytes 2097152 | tf_op jit(solution)/shard_map/reduce-window.4
  66.1 1.5 %fusion.9 = (bf16[512,512]{0,1:T(8,128)(2,1)S(1)}, f32[512]{0:T(512)S(1)}) fusion(f32[512,4,128]{0,2,1:T(8,128)S(1)} %copy.8, f32[512,512]{0,1:T(8,128)S(1)} %get-tuple-element.325, s32[512]{0:T(512)S(1)} %get-tuple-element.326, s32[512]{0:T(512)S(1)} %get-tuple-element.327), kind=kLoop, calls=%fused_computation.23 | loop fusion | flops 5504512 | bytes 2627584 | tf_op jit(solution)/shard_map/while/body/eval_jaxpr/cond/branch_1_fun/convert_element_type | solution.py:34
  68.2 6.3 %collective-permute-done.1 = f32[512]{0:T(512)S(1)} collective-permute-done((f32[512]{0:T(512)S(1)}, f32[512]{0:T(512)S(1)}, u32[]{:S(2)}, u32[]{:S(2)}) %collective-permute-start.1) | collective-permute-done | bytes 2080 | tf_op jit(solution)/shard_map/while/body/eval_jaxpr/ppermute | solution.py:11
  74.5 0.8 %fusion.19 = bf16[1,512,128]{2,1,0:T(8,128)(2,1)} fusion(f32[512,128]{1,0:T(8,128)S(1)} %get-tuple-element.297, f32[512,128]{1,0:T(8,128)S(1)} %get-tuple-element.299, f32[512]{0:T(512)S(1)} %negate_exponential_fusion.1), kind=kLoop, calls=%fused_computation.41 | loop fusion | flops 196608 | bytes 657408 | tf_op jit(solution)/shard_map/stack | solution.py:70
  (54 shorter events, 4.1 us)
Async XLA Ops:
  7.8 1.5 %copy-start.1 = (bf16[512,128]{1,0:T(8,128)(2,1)S(1)}, bf16[512,128]{1,0:T(8,128)(2,1)}, u32[]{:S(2)}) copy-start(bf16[512,128]{1,0:T(8,128)(2,1)} %get-tuple-element.274) | copy-start | bytes 393220 | tf_op jit(solution)/shard_map/cond
  27.4 0.9 %copy-start = (bf16[1,512,128]{2,1,0:T(8,128)(2,1)S(1)}, bf16[1,512,128]{2,1,0:T(8,128)(2,1)}, u32[]{:S(2)}) copy-start(bf16[1,512,128]{2,1,0:T(8,128)(2,1)} %param.12) | copy-start | bytes 393220
  27.4 1.0 %copy-start.2 = (bf16[1,512,128]{2,1,0:T(8,128)(2,1)S(1)}, bf16[1,512,128]{2,1,0:T(8,128)(2,1)}, u32[]{:S(2)}) copy-start(bf16[1,512,128]{2,1,0:T(8,128)(2,1)} %param.11) | copy-start | bytes 393220
  37.2 6.8 %collective-permute-start = (f32[512,128]{1,0:T(8,128)S(1)}, f32[512,128]{1,0:T(8,128)S(1)}, u32[]{:S(2)}, u32[]{:S(2)}) collective-permute-start(f32[512,128]{1,0:T(8,128)S(1)} %multiply_add_fusion.2), channel_id=1, source_target_pairs={{4,0},{8,4},{12,8},{0,12},{5,1},{9,5},{13,9},{1,13},{6,2},{10,6},{... | collective-permute-start | bytes 786440 | tf_op jit(solution)/shard_map/while/body/eval_jaxpr/ppermute | solution.py:11
  37.3 6.7 %collective-permute-start.1 = (f32[512]{0:T(512)S(1)}, f32[512]{0:T(512)S(1)}, u32[]{:S(2)}, u32[]{:S(2)}) collective-permute-start(f32[512]{0:T(512)S(1)} %get-tuple-element.392), channel_id=1, source_target_pairs={{4,0},{8,4},{12,8},{0,12},{5,1},{9,5},{13,9},{1,13},{6,2},{10,6},{... | collective-permute-start | bytes 6152 | tf_op jit(solution)/shard_map/while/body/eval_jaxpr/ppermute | solution.py:11
  52.8 6.5 %collective-permute-start = (f32[512,128]{1,0:T(8,128)S(1)}, f32[512,128]{1,0:T(8,128)S(1)}, u32[]{:S(2)}, u32[]{:S(2)}) collective-permute-start(f32[512,128]{1,0:T(8,128)S(1)} %multiply_add_fusion.2), channel_id=1, source_target_pairs={{4,0},{8,4},{12,8},{0,12},{5,1},{9,5},{13,9},{1,13},{6,2},{10,6},{... | collective-permute-start | bytes 786440 | tf_op jit(solution)/shard_map/while/body/eval_jaxpr/ppermute | solution.py:11
  52.9 6.4 %collective-permute-start.1 = (f32[512]{0:T(512)S(1)}, f32[512]{0:T(512)S(1)}, u32[]{:S(2)}, u32[]{:S(2)}) collective-permute-start(f32[512]{0:T(512)S(1)} %get-tuple-element.392), channel_id=1, source_target_pairs={{4,0},{8,4},{12,8},{0,12},{5,1},{9,5},{13,9},{1,13},{6,2},{10,6},{... | collective-permute-start | bytes 6152 | tf_op jit(solution)/shard_map/while/body/eval_jaxpr/ppermute | solution.py:11
  68.1 6.5 %collective-permute-start = (f32[512,128]{1,0:T(8,128)S(1)}, f32[512,128]{1,0:T(8,128)S(1)}, u32[]{:S(2)}, u32[]{:S(2)}) collective-permute-start(f32[512,128]{1,0:T(8,128)S(1)} %multiply_add_fusion.2), channel_id=1, source_target_pairs={{4,0},{8,4},{12,8},{0,12},{5,1},{9,5},{13,9},{1,13},{6,2},{10,6},{... | collective-permute-start | bytes 786440 | tf_op jit(solution)/shard_map/while/body/eval_jaxpr/ppermute | solution.py:11
  68.2 6.4 %collective-permute-start.1 = (f32[512]{0:T(512)S(1)}, f32[512]{0:T(512)S(1)}, u32[]{:S(2)}, u32[]{:S(2)}) collective-permute-start(f32[512]{0:T(512)S(1)} %get-tuple-element.392), channel_id=1, source_target_pairs={{4,0},{8,4},{12,8},{0,12},{5,1},{9,5},{13,9},{1,13},{6,2},{10,6},{... | collective-permute-start | bytes 6152 | tf_op jit(solution)/shard_map/while/body/eval_jaxpr/ppermute | solution.py:11
where the time goes:
time: 75.5 us; the launch traced here: 75.3 us
  other arithmetic  26.9 us (36%)
  blocking collectives  17.8 us (24%)
  waiting for transfers between devices  17.1 us (23%)
  matrix products  8.32 us (11%)
  starting transfers between devices  2.47 us (3%)
  local copies, waits for them, and re-layouts  2.38 us (3%)
    another operation x8, other arithmetic  19.3 us
    all_gather x1, blocking collectives, one_head(): lax.all_gather(q_own, 'ctx', axis=0, tiled=True).reshape(count, rows, width)  17.8 us
    ppermute x6, waiting for transfers between devices, shifted(): return lax.ppermute(block, axis, route)  17.1 us
    dot_general x4, matrix products, compute(): lax.dot_general(qrows, kblock, (((1,), (1,)), ((), ())), preferred_elemen...  6.95 us
    convert_element_type x4, other arithmetic, compute(): jnp.where(live, jnp.exp(jax.nn.log_sigmoid(score) - later), 0.0)  5.99 us
    ppermute x6, starting transfers between devices, shifted(): return lax.ppermute(block, axis, route)  2.47 us
  transfers between devices with their start and end apart: 6, of which 3 were waited for; matrix products, arithmetic and copies ran while one was open for 0% of the time, Pallas kernels for 0%

commit v1 on v0

--- a/solution.py
+++ b/solution.py
@@ -47,7 +47,30 @@
     count = lax.axis_size("ctx")
     place = lax.axis_index("ctx")
     own_start = place * rows
-    gathered = lax.all_gather(q_own, "ctx", axis=0, tiled=True).reshape(count, rows, width)
+
+    def view_leaf(row_data):
+        all_values = jax.lax.axis_size("ctx")
+        last = jax.lax.axis_index("ctx")
+        step_out, carry_in, moved = (all_values, last, row_data.shape[0])
+        raw_out = tuple((w * step_out if h == 0 else w for h, w in enumerate(row_data.shape)))
+        local_now = jnp.zeros(raw_out, row_data.dtype)
+        parts_out = lax.dynamic_update_slice_in_dim(local_now, row_data, carry_in * moved, axis=0)
+        main = then = row_data
+        for u in tuple(range(1, step_out // 2 + 1)):
+            out_arr = tuple(((h, (h + 1) % step_out) for h in range(step_out)))
+            main = jax.lax.ppermute(main, "ctx", out_arr)
+            parts_out = lax.dynamic_update_slice_in_dim(
+                parts_out, main, (carry_in - u) % step_out * moved, axis=0
+            )
+            if 2 * u < step_out:
+                mixed_arr = tuple(((h, (h - 1) % step_out) for h in range(step_out)))
+                then = jax.lax.ppermute(then, "ctx", mixed_arr)
+                parts_out = lax.dynamic_update_slice_in_dim(
+                    parts_out, then, (carry_in + u) % step_out * moved, axis=0
+                )
+        return parts_out
+
+    gathered = view_leaf(q_own).reshape(count, rows, width)
 
     def advance(step, message):
         summed, spent_sum = message

time: 75.5 us -> 69.9 us (0.926)
  blocking collectives: 17.8 us -> 0 us
  waiting for transfers between devices: 17.1 us -> 25 us
  starting transfers between devices: 2.47 us -> 6.27 us
  local copies, waits for them, and re-layouts: 2.38 us -> 3.68 us
  matrix products: 8.32 us -> 7.35 us
    all_gather x1 -> x0, blocking collectives: 17.8 us -> none  [one_head(): lax.all_gather(q_own, 'ctx', axis=0, tiled=True).reshape(count, rows, width)]
    ppermute x0 -> x3, waiting for transfers between devices: none -> 6.4 us  [the longest x2 6.4 us: view_leaf(): main = jax.lax.ppermute(main, 'ctx', out_arr)]
    ppermute x0 -> x3, starting transfers between devices: none -> 5.32 us  [the longest x2 3.29 us: view_leaf(): main = jax.lax.ppermute(main, 'ctx', out_arr)]
    ppermute x6, starting transfers between devices: 2.47 us -> 0.95 us  [shifted(): return lax.ppermute(block, axis, route)]
    ppermute x6, waiting for transfers between devices: 17.1 us -> 18.6 us  [shifted(): return lax.ppermute(block, axis, route)]
    unnamed x4 -> x10, local copies, waits for them, and re-layouts: 0.94 us -> 2.1 us
    dot_general x4, matrix products: 6.95 us -> 5.99 us  [compute(): lax.dot_general(qrows, kblock, (((1,), (1,)), ((), ())), preferred_elemen...]
  transfers between devices with their start and end apart: 6 -> 9, of which waited for: 3 -> 4; matrix products, arithmetic and copies ran while one was open for 0% -> 13% of each run, Pallas kernels for 0% -> 0%
where the time goes in v1:
time: 69.9 us; the launch traced here: 69.8 us
  other arithmetic  26.9 us (38%)
  waiting for transfers between devices  25 us (36%)
  matrix products  7.35 us (11%)
  starting transfers between devices  6.27 us (9%)
  local copies, waits for them, and re-layouts  3.68 us (5%)
    another operation x8, other arithmetic  19.3 us
    ppermute x6, waiting for transfers between devices, shifted(): return lax.ppermute(block, axis, route)  18.6 us
    ppermute x2, waiting for transfers between devices, view_leaf(): main = jax.lax.ppermute(main, 'ctx', out_arr)  6.4 us
    convert_element_type x4, other arithmetic, compute(): jnp.where(live, jnp.exp(jax.nn.log_sigmoid(score) - later), 0.0)  5.99 us
    dot_general x4, matrix products, compute(): lax.dot_general(qrows, kblock, (((1,), (1,)), ((), ())), preferred_elemen...  5.99 us
    ppermute x2, starting transfers between devices, view_leaf(): main = jax.lax.ppermute(main, 'ctx', out_arr)  3.29 us
    unnamed x10, local copies, waits for them, and re-layouts  2.1 us
    ppermute x1, starting transfers between devices, view_leaf(): then = jax.lax.ppermute(then, 'ctx', mixed_arr)  2.03 us
  transfers between devices with their start and end apart: 9, of which 4 were waited for; matrix products, arithmetic and copies ran while one was open for 13% of the time, Pallas kernels for 0%

profile of v1, /device:TPU:0, one launch (start us, length us, event | category | flops | bytes accessed | tf_op | source)
XLA Modules:
  0.0 69.8 jit_solution(4348678397589914659)
XLA Ops:
  0.0 3.1 %collective-permute-start.2 = (bf16[512,128]{1,0:T(8,128)(2,1)}, bf16[512,128]{1,0:T(8,128)(2,1)S(1)}, u32[]{:S(2)}, u32[]{:S(2)}) collective-permute-start(bf16[512,128]{1,0:T(8,128)(2,1)} %bitcast.50), channel_id=1, source_target_pairs={{0,4},{4,8},{8,12},{12,0},{1,5},{5,9},{9,13},{13,1},{2,6},{6,10},{... | collective-permute-start | bytes 393224 | tf_op jit(solution)/shard_map/ppermute | solution.py:61
  3.1 2.0 %collective-permute-start.3 = (bf16[512,128]{1,0:T(8,128)(2,1)}, bf16[512,128]{1,0:T(8,128)(2,1)S(1)}, u32[]{:S(2)}, u32[]{:S(2)}) collective-permute-start(bf16[512,128]{1,0:T(8,128)(2,1)} %bitcast.51), channel_id=1, source_target_pairs={{0,12},{4,0},{8,4},{12,8},{1,13},{5,1},{9,5},{13,9},{2,14},{6,2},{... | collective-permute-start | bytes 393224 | tf_op jit(solution)/shard_map/ppermute | solution.py:67
  6.0 0.9 %copy-done = bf16[1,512,128]{2,1,0:T(8,128)(2,1)S(1)} copy-done((bf16[1,512,128]{2,1,0:T(8,128)(2,1)S(1)}, bf16[1,512,128]{2,1,0:T(8,128)(2,1)}, u32[]{:S(2)}) %copy-start) | copy-done | bytes 131096
  7.0 8.7 %conditional.2 = (f32[512]{0:T(512)S(1)}, f32[512,128]{1,0:T(8,128)S(1)}) conditional(s32[]{:T(128)} %convert_element_type.23, () %tuple.48, (s32[]{:T(128)}, bf16[512,128]{1,0:T(8,128)(2,1)S(1)}, bf16[512,128]{1,0:T(8,128)(2,1)S(1)}, f32[]{:T(128)}, bf16[512,128]{1,0:T(8,128)(2,1)S(1)}) %tuple.82), branch_computations={%region_0.1_spmd, %region_1.5_spmd} | conditional | flops 175906304 | bytes 12290076 | solution.py:42
  7.0 1.5 %compare_select_fusion.3 = (f32[512,512]{0,1:T(8,128)S(1)}, f32[512,512]{0,1:T(8,128)S(1)}) fusion(s32[512]{0:T(512)S(1)} %iota_add_fusion, f32[]{:T(128)} %get-tuple-element.273, bf16[512,128]{1,0:T(8,128)(2,1)S(1)} %get-tuple-element.271, bf16[512,128]{1,0:T(8,128)(2,1)S(1)} %get-tuple-element.272), kind=kOutput, calls=%fused_computation.5 | convolution fusion | flops 69730304 | bytes 2361348 | tf_op jit(solution)/shard_map/cond/branch_1_fun/dot_general | solution.py:22
  8.5 4.8 %fusion.5 = f32[512,4,128]{0,1,2:T(4,128)S(1)} fusion(f32[512,4,128]{0,2,1:T(8,128)S(1)} %bitcast.48), kind=kOutput, calls=%fused_computation.11 | output fusion | flops 33292288 | bytes 2097152 | tf_op jit(solution)/shard_map/reduce-window.2
  13.8 1.5 %fusion.1 = (bf16[512,512]{0,1:T(8,128)(2,1)S(1)}, f32[512]{0:T(512)S(1)}) fusion(f32[512,4,128]{0,2,1:T(8,128)S(1)} %copy.6, f32[512,512]{0,1:T(8,128)S(1)} %get-tuple-element.321, s32[512]{0:T(512)S(1)} %iota_add_fusion), kind=kLoop, calls=%fused_computation.6 | loop fusion | flops 5504512 | bytes 2625536 | tf_op jit(solution)/shard_map/cond/branch_1_fun/convert_element_type | solution.py:34
  16.3 6.4 %collective-permute-done.4 = bf16[512,128]{1,0:T(8,128)(2,1)S(1)} collective-permute-done((bf16[512,128]{1,0:T(8,128)(2,1)S(1)}, bf16[512,128]{1,0:T(8,128)(2,1)S(1)}, u32[]{:S(2)}, u32[]{:S(2)}) %collective-permute-start.4) | collective-permute-done | bytes 131104 | tf_op jit(solution)/shard_map/ppermute | solution.py:61
  22.8 46.2 %while.17 = (s32[]{:T(128)}, f32[512,128]{1,0:T(8,128)S(1)}, f32[512]{0:T(512)S(1)}, s32[]{:T(128)}, s32[]{:T(128)}, /*index=5*/bf16[4,512,128]{2,1,0:T(8,128)(2...) while((s32[]{:T(128)}, f32[512,128]{1,0:T(8,128)S(1)}, ...), condition=%wide.region_11.12_spmd, body=%wide.region_5.11_spmd.sunk | while | flops 176038928 | bytes 14150142 | solution.py:85
  22.8 8.7 %conditional.4 = (f32[512]{0:T(512)S(1)}, f32[512,128]{1,0:T(8,128)S(1)}) conditional(s32[]{:T(128)} %convert_element_type.31, () %tuple.69, (s32[]{:T(128)}, s32[]{:T(128)}, s32[]{:T(128)}, bf16[4,512,128]{2,1,0:T(8,128)(2,1)S(1)}, bf16[512,128]{1,0:T(8,128)(2,1)S(1)}, /*index=5*/f32[]{:T(128)}, bf16[512,128]{1,0:T(8,128)(2,1)S(1)}) %tuple.70), branch_computations={%region_6.6_spmd, %region_7.10_spmd} | conditional | flops 175906816 | bytes 12296262 | solution.py:42
  22.9 1.5 %compare_select_fusion.7 = (f32[512,512]{0,1:T(8,128)S(1)}, f32[512,512]{0,1:T(8,128)S(1)}) fusion(s32[512]{0:T(512)S(1)} %get-tuple-element.326, s32[512]{0:T(512)S(1)} %get-tuple-element.327, f32[]{:T(128)} %get-tuple-element.280, bf16[512,128]{1,0:T(8,128)(2,1)S(1)} %get-tuple-element.279, bf16[4,512,128]{2,1,0:T(8,128)(2,1)S(1)} %get-tuple-element.277, ...), kind=kOutput, calls=%fused_computation.22 | convolution fusion | flops 69730304 | bytes 2363400 | tf_op jit(solution)/shard_map/while/body/eval_jaxpr/cond/branch_1_fun/dot_general | solution.py:22
  24.4 4.8 %fusion.13 = f32[512,4,128]{0,1,2:T(4,128)S(1)} fusion(f32[512,4,128]{0,2,1:T(8,128)S(1)} %bitcast.42), kind=kOutput, calls=%fused_computation.28 | output fusion | flops 33292288 | bytes 2097152 | tf_op jit(solution)/shard_map/reduce-window.4
  29.7 1.5 %fusion.9 = (bf16[512,512]{0,1:T(8,128)(2,1)S(1)}, f32[512]{0:T(512)S(1)}) fusion(f32[512,4,128]{0,2,1:T(8,128)S(1)} %copy.8, f32[512,512]{0,1:T(8,128)S(1)} %get-tuple-element.325, s32[512]{0:T(512)S(1)} %get-tuple-element.326, s32[512]{0:T(512)S(1)} %get-tuple-element.327), kind=kLoop, calls=%fused_computation.23 | loop fusion | flops 5504512 | bytes 2627584 | tf_op jit(solution)/shard_map/while/body/eval_jaxpr/cond/branch_1_fun/convert_element_type | solution.py:34
  32.4 6.0 %collective-permute-done.1 = f32[512]{0:T(512)S(1)} collective-permute-done((f32[512]{0:T(512)S(1)}, f32[512]{0:T(512)S(1)}, u32[]{:S(2)}, u32[]{:S(2)}) %collective-permute-start.1) | collective-permute-done | bytes 2080 | tf_op jit(solution)/shard_map/while/body/eval_jaxpr/ppermute | solution.py:11
  38.4 8.7 %conditional.4 = (f32[512]{0:T(512)S(1)}, f32[512,128]{1,0:T(8,128)S(1)}) conditional(s32[]{:T(128)} %convert_element_type.31, () %tuple.69, (s32[]{:T(128)}, s32[]{:T(128)}, s32[]{:T(128)}, bf16[4,512,128]{2,1,0:T(8,128)(2,1)S(1)}, bf16[512,128]{1,0:T(8,128)(2,1)S(1)}, /*index=5*/f32[]{:T(128)}, bf16[512,128]{1,0:T(8,128)(2,1)S(1)}) %tuple.70), branch_computations={%region_6.6_spmd, %region_7.10_spmd} | conditional | flops 175906816 | bytes 12296262 | solution.py:42
  38.4 1.5 %compare_select_fusion.7 = (f32[512,512]{0,1:T(8,128)S(1)}, f32[512,512]{0,1:T(8,128)S(1)}) fusion(s32[512]{0:T(512)S(1)} %get-tuple-element.326, s32[512]{0:T(512)S(1)} %get-tuple-element.327, f32[]{:T(128)} %get-tuple-element.280, bf16[512,128]{1,0:T(8,128)(2,1)S(1)} %get-tuple-element.279, bf16[4,512,128]{2,1,0:T(8,128)(2,1)S(1)} %get-tuple-element.277, ...), kind=kOutput, calls=%fused_computation.22 | convolution fusion | flops 69730304 | bytes 2363400 | tf_op jit(solution)/shard_map/while/body/eval_jaxpr/cond/branch_1_fun/dot_general | solution.py:22
  39.9 4.8 %fusion.13 = f32[512,4,128]{0,1,2:T(4,128)S(1)} fusion(f32[512,4,128]{0,2,1:T(8,128)S(1)} %bitcast.42), kind=kOutput, calls=%fused_computation.28 | output fusion | flops 33292288 | bytes 2097152 | tf_op jit(solution)/shard_map/reduce-window.4
  45.2 1.5 %fusion.9 = (bf16[512,512]{0,1:T(8,128)(2,1)S(1)}, f32[512]{0:T(512)S(1)}) fusion(f32[512,4,128]{0,2,1:T(8,128)S(1)} %copy.8, f32[512,512]{0,1:T(8,128)S(1)} %get-tuple-element.325, s32[512]{0:T(512)S(1)} %get-tuple-element.326, s32[512]{0:T(512)S(1)} %get-tuple-element.327), kind=kLoop, calls=%fused_computation.23 | loop fusion | flops 5504512 | bytes 2627584 | tf_op jit(solution)/shard_map/while/body/eval_jaxpr/cond/branch_1_fun/convert_element_type | solution.py:34
  47.4 6.3 %collective-permute-done.1 = f32[512]{0:T(512)S(1)} collective-permute-done((f32[512]{0:T(512)S(1)}, f32[512]{0:T(512)S(1)}, u32[]{:S(2)}, u32[]{:S(2)}) %collective-permute-start.1) | collective-permute-done | bytes 2080 | tf_op jit(solution)/shard_map/while/body/eval_jaxpr/ppermute | solution.py:11
  53.7 8.7 %conditional.4 = (f32[512]{0:T(512)S(1)}, f32[512,128]{1,0:T(8,128)S(1)}) conditional(s32[]{:T(128)} %convert_element_type.31, () %tuple.69, (s32[]{:T(128)}, s32[]{:T(128)}, s32[]{:T(128)}, bf16[4,512,128]{2,1,0:T(8,128)(2,1)S(1)}, bf16[512,128]{1,0:T(8,128)(2,1)S(1)}, /*index=5*/f32[]{:T(128)}, bf16[512,128]{1,0:T(8,128)(2,1)S(1)}) %tuple.70), branch_computations={%region_6.6_spmd, %region_7.10_spmd} | conditional | flops 175906816 | bytes 12296262 | solution.py:42
  53.7 1.5 %compare_select_fusion.7 = (f32[512,512]{0,1:T(8,128)S(1)}, f32[512,512]{0,1:T(8,128)S(1)}) fusion(s32[512]{0:T(512)S(1)} %get-tuple-element.326, s32[512]{0:T(512)S(1)} %get-tuple-element.327, f32[]{:T(128)} %get-tuple-element.280, bf16[512,128]{1,0:T(8,128)(2,1)S(1)} %get-tuple-element.279, bf16[4,512,128]{2,1,0:T(8,128)(2,1)S(1)} %get-tuple-element.277, ...), kind=kOutput, calls=%fused_computation.22 | convolution fusion | flops 69730304 | bytes 2363400 | tf_op jit(solution)/shard_map/while/body/eval_jaxpr/cond/branch_1_fun/dot_general | solution.py:22
  55.2 4.8 %fusion.13 = f32[512,4,128]{0,1,2:T(4,128)S(1)} fusion(f32[512,4,128]{0,2,1:T(8,128)S(1)} %bitcast.42), kind=kOutput, calls=%fused_computation.28 | output fusion | flops 33292288 | bytes 2097152 | tf_op jit(solution)/shard_map/reduce-window.4
  60.5 1.5 %fusion.9 = (bf16[512,512]{0,1:T(8,128)(2,1)S(1)}, f32[512]{0:T(512)S(1)}) fusion(f32[512,4,128]{0,2,1:T(8,128)S(1)} %copy.8, f32[512,512]{0,1:T(8,128)S(1)} %get-tuple-element.325, s32[512]{0:T(512)S(1)} %get-tuple-element.326, s32[512]{0:T(512)S(1)} %get-tuple-element.327), kind=kLoop, calls=%fused_computation.23 | loop fusion | flops 5504512 | bytes 2627584 | tf_op jit(solution)/shard_map/while/body/eval_jaxpr/cond/branch_1_fun/convert_element_type | solution.py:34
  62.6 6.3 %collective-permute-done.1 = f32[512]{0:T(512)S(1)} collective-permute-done((f32[512]{0:T(512)S(1)}, f32[512]{0:T(512)S(1)}, u32[]{:S(2)}, u32[]{:S(2)}) %collective-permute-start.1) | collective-permute-done | bytes 2080 | tf_op jit(solution)/shard_map/while/body/eval_jaxpr/ppermute | solution.py:11
  (68 shorter events, 7.1 us)
Async XLA Ops:
  0.0 15.7 %collective-permute-start.2 = (bf16[512,128]{1,0:T(8,128)(2,1)}, bf16[512,128]{1,0:T(8,128)(2,1)S(1)}, u32[]{:S(2)}, u32[]{:S(2)}) collective-permute-start(bf16[512,128]{1,0:T(8,128)(2,1)} %bitcast.50), channel_id=1, source_target_pairs={{0,4},{4,8},{8,12},{12,0},{1,5},{5,9},{9,13},{13,1},{2,6},{6,10},{... | collective-permute-start | bytes 393224 | tf_op jit(solution)/shard_map/ppermute | solution.py:61
  3.1 13.0 %collective-permute-start.3 = (bf16[512,128]{1,0:T(8,128)(2,1)}, bf16[512,128]{1,0:T(8,128)(2,1)S(1)}, u32[]{:S(2)}, u32[]{:S(2)}) collective-permute-start(bf16[512,128]{1,0:T(8,128)(2,1)} %bitcast.51), channel_id=1, source_target_pairs={{0,12},{4,0},{8,4},{12,8},{1,13},{5,1},{9,5},{13,9},{2,14},{6,2},{... | collective-permute-start | bytes 393224 | tf_op jit(solution)/shard_map/ppermute | solution.py:67
  5.1 0.9 %copy-start.3 = (bf16[1,512,128]{2,1,0:T(8,128)(2,1)S(1)}, bf16[1,512,128]{2,1,0:T(8,128)(2,1)}, u32[]{:S(2)}) copy-start(bf16[1,512,128]{2,1,0:T(8,128)(2,1)} %param.10) | copy-start | bytes 393220
  6.0 0.9 %copy-start = (bf16[1,512,128]{2,1,0:T(8,128)(2,1)S(1)}, bf16[1,512,128]{2,1,0:T(8,128)(2,1)}, u32[]{:S(2)}) copy-start(bf16[1,512,128]{2,1,0:T(8,128)(2,1)} %param.12) | copy-start | bytes 393220
  6.0 1.0 %copy-start.4 = (bf16[1,512,128]{2,1,0:T(8,128)(2,1)S(1)}, bf16[1,512,128]{2,1,0:T(8,128)(2,1)}, u32[]{:S(2)}) copy-start(bf16[1,512,128]{2,1,0:T(8,128)(2,1)} %param.11) | copy-start | bytes 393220
  15.6 0.7 copy-start.1
  15.7 7.0 %collective-permute-start.4 = (bf16[512,128]{1,0:T(8,128)(2,1)S(1)}, bf16[512,128]{1,0:T(8,128)(2,1)S(1)}, u32[]{:S(2)}, u32[]{:S(2)}) collective-permute-start(bf16[512,128]{1,0:T(8,128)(2,1)S(1)} %collective-permute-done.2), channel_id=1, source_target_pairs={{0,4},{4,8},{8,12},{12,0},{1,5},{5,9},{9,13},{13,1},{2,6},{6,10},{... | collective-permute-start | bytes 393224 | tf_op jit(solution)/shard_map/ppermute | solution.py:61
  22.8 46.2 %copy-start.2 = (f32[512,128]{1,0:T(8,128)S(1)}, f32[512,128]{1,0:T(8,128)}, u32[]{:S(2)}) copy-start(f32[512,128]{1,0:T(8,128)} %copy-done.1) | copy-start | bytes 786436
  31.7 6.7 %collective-permute-start = (f32[512,128]{1,0:T(8,128)S(1)}, f32[512,128]{1,0:T(8,128)S(1)}, u32[]{:S(2)}, u32[]{:S(2)}) collective-permute-start(f32[512,128]{1,0:T(8,128)S(1)} %multiply_add_fusion.2), channel_id=1, source_target_pairs={{4,0},{8,4},{12,8},{0,12},{5,1},{9,5},{13,9},{1,13},{6,2},{10,6},{... | collective-permute-start | bytes 786440 | tf_op jit(solution)/shard_map/while/body/eval_jaxpr/ppermute | solution.py:11
  31.8 6.6 %collective-permute-start.1 = (f32[512]{0:T(512)S(1)}, f32[512]{0:T(512)S(1)}, u32[]{:S(2)}, u32[]{:S(2)}) collective-permute-start(f32[512]{0:T(512)S(1)} %get-tuple-element.392), channel_id=1, source_target_pairs={{4,0},{8,4},{12,8},{0,12},{5,1},{9,5},{13,9},{1,13},{6,2},{10,6},{... | collective-permute-start | bytes 6152 | tf_op jit(solution)/shard_map/while/body/eval_jaxpr/ppermute | solution.py:11
  47.2 6.5 %collective-permute-start = (f32[512,128]{1,0:T(8,128)S(1)}, f32[512,128]{1,0:T(8,128)S(1)}, u32[]{:S(2)}, u32[]{:S(2)}) collective-permute-start(f32[512,128]{1,0:T(8,128)S(1)} %multiply_add_fusion.2), channel_id=1, source_target_pairs={{4,0},{8,4},{12,8},{0,12},{5,1},{9,5},{13,9},{1,13},{6,2},{10,6},{... | collective-permute-start | bytes 786440 | tf_op jit(solution)/shard_map/while/body/eval_jaxpr/ppermute | solution.py:11
  47.3 6.4 %collective-permute-start.1 = (f32[512]{0:T(512)S(1)}, f32[512]{0:T(512)S(1)}, u32[]{:S(2)}, u32[]{:S(2)}) collective-permute-start(f32[512]{0:T(512)S(1)} %get-tuple-element.392), channel_id=1, source_target_pairs={{4,0},{8,4},{12,8},{0,12},{5,1},{9,5},{13,9},{1,13},{6,2},{10,6},{... | collective-permute-start | bytes 6152 | tf_op jit(solution)/shard_map/while/body/eval_jaxpr/ppermute | solution.py:11
  62.5 6.5 %collective-permute-start = (f32[512,128]{1,0:T(8,128)S(1)}, f32[512,128]{1,0:T(8,128)S(1)}, u32[]{:S(2)}, u32[]{:S(2)}) collective-permute-start(f32[512,128]{1,0:T(8,128)S(1)} %multiply_add_fusion.2), channel_id=1, source_target_pairs={{4,0},{8,4},{12,8},{0,12},{5,1},{9,5},{13,9},{1,13},{6,2},{10,6},{... | collective-permute-start | bytes 786440 | tf_op jit(solution)/shard_map/while/body/eval_jaxpr/ppermute | solution.py:11
  62.6 6.4 %collective-permute-start.1 = (f32[512]{0:T(512)S(1)}, f32[512]{0:T(512)S(1)}, u32[]{:S(2)}, u32[]{:S(2)}) collective-permute-start(f32[512]{0:T(512)S(1)} %get-tuple-element.392), channel_id=1, source_target_pairs={{4,0},{8,4},{12,8},{0,12},{5,1},{9,5},{13,9},{1,13},{6,2},{10,6},{... | collective-permute-start | bytes 6152 | tf_op jit(solution)/shard_map/while/body/eval_jaxpr/ppermute | solution.py:11
